TPU v7x, 256 devices: a whole 4x4x8 slice. The times are simulated.
256 devices in a mesh: ctx: 32 (over x, y, core), tp: 8 (over z).
Axes of the slice: x: 4, y: 4, z: 8, core: 2. Of those that a mesh axis runs over, the one named last changes fastest.
Arguments:
- hidden_states: bfloat16 [65536, 4096], P('ctx', 'tp')
- chosen: int32 [12288], P('ctx'), may hold values from 0 to 2048, as said below
- router_gate: float32 [12288], P('ctx'), may hold values from 0.2 to 1
- w_query: bfloat16 [4096, 4096], P(None, 'tp'), may hold values from -0.09375 to 0.09375
- w_key: bfloat16 [4096, 1024], P(None, 'tp'), may hold values from -0.09375 to 0.09375
- w_value: bfloat16 [4096, 1024], P(None, 'tp'), may hold values from -0.09375 to 0.09375
Outputs:
- attended: bfloat16 [12288, 4096], P('ctx', 'tp')
Inputs may be any that keep to these rules, and one draw needn't show every extreme that they name: `chosen`: each shard's 384 slots hold the sorted distinct positions of its routed tokens, then 2048 in every unused slot; a shard routes from 128 to 384 tokens, some shard exactly 384, and all shards together 65536 // 8.
All inputs are finite; a program needn't handle non-finite values.
Results may differ from a plain program's by a relative error of at most 0.035.
Values may be sent and summed in bfloat16 or wider, within the bound.
No kernel may reach another device: no remote copies, remote signals or barrier semaphores. Data moves between devices by JAX's collectives and lax.ppermute only.
A program may use at most 64 MiB of HBM per device.

v0:
```python
import math
import jax
import jax.numpy as jnp
from jax import lax
from jax.sharding import PartitionSpec as P

HEAD_DIM = 128
ROPE_BASE = 500000.0
MASKED = -1e30


def rotate(values_in, position):
    half_dim = values_in.shape[-1] // 2
    frequency = jnp.exp(
        jnp.arange(half_dim, dtype=jnp.float32) * (-2.0 * math.log(ROPE_BASE) / values_in.shape[-1])
    )
    angles = position.astype(jnp.float32)[:, None] * frequency[None, :]
    cosine = jnp.cos(angles)[:, None, :]
    sine = jnp.sin(angles)[:, None, :]
    first = values_in[..., :half_dim]
    second = values_in[..., half_dim:]
    return jnp.concatenate(
        [first * cosine - second * sine, second * cosine + first * sine], axis=-1
    )


def empty_state(count, kv_local, group, head_dim):
    return (
        jnp.full((kv_local, group, count), MASKED, jnp.float32),
        jnp.zeros((kv_local, group, count), jnp.float32),
        jnp.zeros((count, kv_local, group, head_dim), jnp.float32),
    )


def update(state, queries, query_pos, key_block, value_block, key_pos):
    running, totals, summed = state
    scores = jnp.einsum("rhgd,khd->hgrk", queries, key_block, preferred_element_type=jnp.float32)
    allowed = key_pos[None, None, None, :] <= query_pos[None, None, :, None]
    newest = jnp.maximum(running, jnp.max(jnp.where(allowed, scores, MASKED), axis=-1))
    factor = jnp.exp(running - newest)
    weights = jnp.where(allowed, jnp.exp(scores - newest[..., None]), 0.0)
    totals = totals * factor + jnp.sum(weights, axis=-1)
    mixed = jnp.einsum(
        "hgrk,khd->rhgd",
        weights.astype(jnp.bfloat16),
        value_block,
        preferred_element_type=jnp.float32,
    )
    summed = summed * jnp.transpose(factor, (2, 0, 1))[..., None] + mixed
    return (newest, totals, summed)


def finish(state):
    running, totals, summed = state
    denom = jnp.where(totals > 0.0, totals, 1.0)
    return summed / jnp.transpose(denom, (2, 0, 1))[..., None]


def highest(position, pad_mark):
    return jnp.max(jnp.where(position < pad_mark, position, -1))


def fold_keys(states, pieces, groups):
    key_rows, value_rows, key_pos = pieces
    length = key_rows.shape[0]
    block_rows = length
    for size_rows in (1536, 768, 384):
        block_rows = size_rows
        break
    blocks = length // block_rows
    shaped = (
        key_rows.reshape((blocks, block_rows) + key_rows.shape[1:]),
        value_rows.reshape((blocks, block_rows) + value_rows.shape[1:]),
        key_pos.reshape(blocks, block_rows),
    )

    def advance(carried, block):
        key_block, value_block, block_pos = block
        fresh = []
        for state, group_data in zip(carried, groups):
            queries, query_pos, limit = group_data

            def visit(current):
                return update(current, queries, query_pos, key_block, value_block, block_pos)

            def keep_state(current):
                return current

            fresh.append(lax.cond(jnp.min(block_pos) > limit, keep_state, visit, state))
        return (tuple(fresh), None)

    result, unused = lax.scan(advance, tuple(states), shaped)
    return result


def body(hidden_states, chosen, router_gate, w_query, w_key, w_value):
    seq_rows = hidden_states.shape[0]
    slot_count = chosen.shape[0]
    head_dim = HEAD_DIM
    query_width = w_query.shape[1]
    kv_width = w_key.shape[1]
    kv_local = kv_width // head_dim
    heads_local = query_width // head_dim
    group = heads_local // kv_local
    live = chosen < seq_rows
    pad_mark = lax.axis_size("ctx") * seq_rows + 1
    position = jnp.where(live, lax.axis_index("ctx") * seq_rows + chosen, pad_mark)
    picked = hidden_states[jnp.minimum(chosen, seq_rows - 1)]
    gated = jnp.where(live, router_gate, 0.0)
    piece = lax.all_gather(picked, "tp", axis=1, tiled=True)
    query_part = jnp.dot(piece, w_query, preferred_element_type=jnp.float32)
    key_part = jnp.dot(piece, w_key, preferred_element_type=jnp.float32)
    value_part = jnp.dot(piece, w_value, preferred_element_type=jnp.float32)
    queries = (
        rotate(query_part.reshape(slot_count, heads_local, head_dim), position) * head_dim ** (-0.5)
    ).astype(jnp.bfloat16)
    queries = queries.reshape(slot_count, kv_local, group, head_dim)
    key_rows = rotate(key_part.reshape(slot_count, kv_local, head_dim), position).astype(
        jnp.bfloat16
    )
    value_rows = value_part.reshape(slot_count, kv_local, head_dim).astype(jnp.bfloat16)
    groups = [(queries, position, highest(position, pad_mark))]
    states = fold_keys(
        (empty_state(slot_count, kv_local, group, head_dim),),
        (
            lax.all_gather(key_rows, "ctx", axis=0, tiled=True),
            lax.all_gather(value_rows, "ctx", axis=0, tiled=True),
            lax.all_gather(position, "ctx", axis=0, tiled=True),
        ),
        groups,
    )
    result = (finish(states[0]) * gated[:, None, None, None]).astype(jnp.bfloat16)
    return result.reshape(slot_count, query_width)


def solution(mesh):
    placed = (P("ctx", "tp"), P("ctx"), P("ctx"), P(None, "tp"), P(None, "tp"), P(None, "tp"))
    return jax.shard_map(
        body, mesh=mesh, in_specs=placed, out_specs=P("ctx", "tp"), check_vma=False
    )
```

profile of v0, /device:TPU:23, one launch (start us, length us, event | category | flops | bytes accessed | tf_op | source)
XLA Modules:
  0.0 253.6 jit_solution(8523070852562474726)
XLA Ops:
  8.1 2.6 %gather_fusion = bf16[384,512]{1,0:T(8,128)(2,1)} fusion(bf16[2048,512]{1,0:T(8,128)(2,1)S(1)} %copy-done, s32[1024]{0:T(1024)S(1)} %pad_clamp_fusion), kind=kCustom, calls=%fused_computation | custom fusion | bytes 787968 | tf_op jit(solution)/shard_map/gather | solution.py:108
  10.8 47.3 %all-gather.9.cloned.1.call-done = bf16[384,4096]{1,0:T(8,128)(2,1)} async-done(((bf16[384,512]{1,0:T(8,128)(2,1)}), bf16[384,4096]{1,0:T(8,128)(2,1)}) %all-gather.9.cloned.1.call-update) | async-done | bytes 3145744 | tf_op jit(solution)/shard_map/all_gather | solution.py:110
  58.1 3.5 %convolution_convert_fusion = bf16[384,128]{1,0:T(8,128)(2,1)} fusion(bf16[384,4096]{1,0:T(8,128)(2,1)} %all-gather.9.cloned.1.call-done, bf16[4096,128]{1,0:T(8,128)(2,1)S(1)} %copy-done.1), kind=kOutput, calls=%fused_computation.29 | convolution fusion | flops 402702336 | bytes 4292608 | tf_op jit(solution)/shard_map/dot_general | solution.py:113
  61.6 3.2 %convolution_bitcast_fusion = f32[384,1,128]{0,2,1:T(8,128)S(1)} fusion(bf16[384,4096]{1,0:T(8,128)(2,1)} %all-gather.9.cloned.1.call-done, bf16[4096,128]{1,0:T(8,128)(2,1)} %param.14), kind=kOutput, calls=%fused_computation.28 | convolution fusion | flops 402653184 | bytes 4390912 | tf_op jit(solution)/shard_map/dot_general | solution.py:112
  66.0 23.6 %all-gather.2 = s32[32,1,384]{2,1,0:T(1,128)S(1)} all-gather(s32[1,1,384]{2,1,0:T(1,128)S(1)} %reshape.287), channel_id=1, replica_groups=mesh['ctx'=32,'tp'=8] {'ctx'}, dimensions={0}, use_global_device_ids=true | all-gather | bytes 50688 | tf_op jit(solution)/shard_map/all_gather | solution.py:128
  91.2 5.8 %fusion.39 = f32[384,512]{1,0:T(8,128)} fusion(bf16[384,4096]{1,0:T(8,128)(2,1)} %all-gather.9.cloned.1.call-done, bf16[4096,512]{1,0:T(8,128)(2,1)} %param.13), kind=kOutput, calls=%fused_computation.61 | convolution fusion | flops 1610612736 | bytes 8126464 | tf_op jit(solution)/shard_map/dot_general | solution.py:111
  99.3 10.0 %all-gather.11.cloned.1.call-done = bf16[12288,128]{1,0:T(8,128)(2,1)} async-done(((bf16[384,128]{1,0:T(8,128)(2,1)}), bf16[12288,128]{1,0:T(8,128)(2,1)}) %all-gather.11.cloned.1.call-update) | async-done | bytes 3145744 | tf_op jit(solution)/shard_map/all_gather | solution.py:127
  109.3 4.6 %copy.17 = bf16[8,1536,1,128]{1,3,2,0:T(8,128)(2,1)} copy(bf16[8,1536,1,128]{3,1,0,2:T(8,128)(2,1)} %bitcast.82) | data formatting | bytes 6291456 | tf_op jit(solution)/shard_map/while | solution.py:92
  113.9 48.9 %all-gather.7.cloned.1.call-done = bf16[12288,1,128]{0,2,1:T(8,128)(2,1)} async-done(((bf16[384,1,128]{0,2,1:T(8,128)(2,1)}), bf16[12288,1,128]{0,2,1:T(8,128)(2,1)}) %all-gather.7.cloned.1.call-update) | async-done | bytes 3145744 | tf_op jit(solution)/shard_map/all_gather | solution.py:126
  162.8 4.6 %copy.20 = bf16[12288,1,128]{2,0,1:T(8,128)(2,1)} copy(bf16[12288,1,128]{0,2,1:T(8,128)(2,1)} %all-gather.7.cloned.1.call-done) | data formatting | bytes 6291456 | tf_op jit(solution)/shard_map/while | solution.py:92
  167.5 78.5 %while.14 = (s32[]{:T(128)}, f32[1,4,384]{2,1,0:T(4,128)S(1)}, f32[1,4,384]{2,1,0:T(4,128)S(1)}, f32[384,1,4,128]{0,3,2,1:T(8,128)S(1)}, s32[8,1536]{1,0:T(8,128...) while((s32[]{:T(128)}, f32[1,4,384]{2,1,0:T(4,128)S(1)}, ...), condition=%wide.region_7.8_spmd, body=%wide.region_1.7_spmd.sunk | while | flops 1227823104 | bytes 33555200 | solution.py:92
  169.5 7.9 %conditional.2 = (f32[1,4,384]{2,1,0:T(4,128)S(1)}, f32[1,4,384]{2,1,0:T(4,128)S(1)}, f32[384,1,4,128]{0,3,2,1:T(8,128)S(1)}) conditional(s32[]{:T(128)} %convert_element_type.58, (s32[1,1536]{1,0:T(1,128)S(1)}, s32[384]{0:T(512)S(1)}, bf16[8,1536,1,128]{3,1,2,0:T(8,128)(2,1)}, s32[]{:T(128)}, bf16[384,1,4,128]{3,0,2,1:T(8,128)(2,1)S(1)}, ...), branch_computations={%region_3.5_spmd, %region_6.6_spmd} | conditional | flops 1227821568 | bytes 33530396 | solution.py:89
  169.9 2.5 fusion
  174.2 3.2 %fusion.12 = f32[384,1,4,128]{0,3,2,1:T(8,128)S(1)} fusion(f32[1536,384,4]{1,0,2:T(8,128)S(1)} %get-tuple-element.191, f32[4,384]{1,0:T(4,128)S(1)} %bitcast.84, pred[384,1536]{0,1:T(8,128)(4,1)S(1)} %broadcast_compare_fusion, f32[384,1,4,128]{0,3,2,1:T(8,128)S(1)} %get-tuple-element.124, bf16[8,1536,1,128]{1,3,2,0:T(8,128)(2,1)} %get-tuple-element.125, ...), kind=kOutput, calls=%fused_computation.12 | convolution fusion | flops 611450880 | bytes 12005888 | tf_op jit(solution)/shard_map/while/body/eval_jaxpr/cond/branch_0_fun/hgrk,khd->rhgd/dot_general | solution.py:43
  179.3 7.9 %conditional.2 = (f32[1,4,384]{2,1,0:T(4,128)S(1)}, f32[1,4,384]{2,1,0:T(4,128)S(1)}, f32[384,1,4,128]{0,3,2,1:T(8,128)S(1)}) conditional(s32[]{:T(128)} %convert_element_type.58, (s32[1,1536]{1,0:T(1,128)S(1)}, s32[384]{0:T(512)S(1)}, bf16[8,1536,1,128]{3,1,2,0:T(8,128)(2,1)}, s32[]{:T(128)}, bf16[384,1,4,128]{3,0,2,1:T(8,128)(2,1)S(1)}, ...), branch_computations={%region_3.5_spmd, %region_6.6_spmd} | conditional | flops 1227821568 | bytes 33530396 | solution.py:89
  179.7 2.5 fusion
  184.0 3.2 %fusion.12 = f32[384,1,4,128]{0,3,2,1:T(8,128)S(1)} fusion(f32[1536,384,4]{1,0,2:T(8,128)S(1)} %get-tuple-element.191, f32[4,384]{1,0:T(4,128)S(1)} %bitcast.84, pred[384,1536]{0,1:T(8,128)(4,1)S(1)} %broadcast_compare_fusion, f32[384,1,4,128]{0,3,2,1:T(8,128)S(1)} %get-tuple-element.124, bf16[8,1536,1,128]{1,3,2,0:T(8,128)(2,1)} %get-tuple-element.125, ...), kind=kOutput, calls=%fused_computation.12 | convolution fusion | flops 611450880 | bytes 12005888 | tf_op jit(solution)/shard_map/while/body/eval_jaxpr/cond/branch_0_fun/hgrk,khd->rhgd/dot_general | solution.py:43
  189.1 7.9 %conditional.2 = (f32[1,4,384]{2,1,0:T(4,128)S(1)}, f32[1,4,384]{2,1,0:T(4,128)S(1)}, f32[384,1,4,128]{0,3,2,1:T(8,128)S(1)}) conditional(s32[]{:T(128)} %convert_element_type.58, (s32[1,1536]{1,0:T(1,128)S(1)}, s32[384]{0:T(512)S(1)}, bf16[8,1536,1,128]{3,1,2,0:T(8,128)(2,1)}, s32[]{:T(128)}, bf16[384,1,4,128]{3,0,2,1:T(8,128)(2,1)S(1)}, ...), branch_computations={%region_3.5_spmd, %region_6.6_spmd} | conditional | flops 1227821568 | bytes 33530396 | solution.py:89
  193.8 3.2 %fusion.12 = f32[384,1,4,128]{0,3,2,1:T(8,128)S(1)} fusion(f32[1536,384,4]{1,0,2:T(8,128)S(1)} %get-tuple-element.191, f32[4,384]{1,0:T(4,128)S(1)} %bitcast.84, pred[384,1536]{0,1:T(8,128)(4,1)S(1)} %broadcast_compare_fusion, f32[384,1,4,128]{0,3,2,1:T(8,128)S(1)} %get-tuple-element.124, bf16[8,1536,1,128]{1,3,2,0:T(8,128)(2,1)} %get-tuple-element.125, ...), kind=kOutput, calls=%fused_computation.12 | convolution fusion | flops 611450880 | bytes 12005888 | tf_op jit(solution)/shard_map/while/body/eval_jaxpr/cond/branch_0_fun/hgrk,khd->rhgd/dot_general | solution.py:43
  198.9 7.9 %conditional.2 = (f32[1,4,384]{2,1,0:T(4,128)S(1)}, f32[1,4,384]{2,1,0:T(4,128)S(1)}, f32[384,1,4,128]{0,3,2,1:T(8,128)S(1)}) conditional(s32[]{:T(128)} %convert_element_type.58, (s32[1,1536]{1,0:T(1,128)S(1)}, s32[384]{0:T(512)S(1)}, bf16[8,1536,1,128]{3,1,2,0:T(8,128)(2,1)}, s32[]{:T(128)}, bf16[384,1,4,128]{3,0,2,1:T(8,128)(2,1)S(1)}, ...), branch_computations={%region_3.5_spmd, %region_6.6_spmd} | conditional | flops 1227821568 | bytes 33530396 | solution.py:89
  199.3 2.5 fusion
  203.6 3.2 %fusion.12 = f32[384,1,4,128]{0,3,2,1:T(8,128)S(1)} fusion(f32[1536,384,4]{1,0,2:T(8,128)S(1)} %get-tuple-element.191, f32[4,384]{1,0:T(4,128)S(1)} %bitcast.84, pred[384,1536]{0,1:T(8,128)(4,1)S(1)} %broadcast_compare_fusion, f32[384,1,4,128]{0,3,2,1:T(8,128)S(1)} %get-tuple-element.124, bf16[8,1536,1,128]{1,3,2,0:T(8,128)(2,1)} %get-tuple-element.125, ...), kind=kOutput, calls=%fused_computation.12 | convolution fusion | flops 611450880 | bytes 12005888 | tf_op jit(solution)/shard_map/while/body/eval_jaxpr/cond/branch_0_fun/hgrk,khd->rhgd/dot_general | solution.py:43
  208.7 7.9 %conditional.2 = (f32[1,4,384]{2,1,0:T(4,128)S(1)}, f32[1,4,384]{2,1,0:T(4,128)S(1)}, f32[384,1,4,128]{0,3,2,1:T(8,128)S(1)}) conditional(s32[]{:T(128)} %convert_element_type.58, (s32[1,1536]{1,0:T(1,128)S(1)}, s32[384]{0:T(512)S(1)}, bf16[8,1536,1,128]{3,1,2,0:T(8,128)(2,1)}, s32[]{:T(128)}, bf16[384,1,4,128]{3,0,2,1:T(8,128)(2,1)S(1)}, ...), branch_computations={%region_3.5_spmd, %region_6.6_spmd} | conditional | flops 1227821568 | bytes 33530396 | solution.py:89
  209.2 2.5 fusion
  213.4 3.2 %fusion.12 = f32[384,1,4,128]{0,3,2,1:T(8,128)S(1)} fusion(f32[1536,384,4]{1,0,2:T(8,128)S(1)} %get-tuple-element.191, f32[4,384]{1,0:T(4,128)S(1)} %bitcast.84, pred[384,1536]{0,1:T(8,128)(4,1)S(1)} %broadcast_compare_fusion, f32[384,1,4,128]{0,3,2,1:T(8,128)S(1)} %get-tuple-element.124, bf16[8,1536,1,128]{1,3,2,0:T(8,128)(2,1)} %get-tuple-element.125, ...), kind=kOutput, calls=%fused_computation.12 | convolution fusion | flops 611450880 | bytes 12005888 | tf_op jit(solution)/shard_map/while/body/eval_jaxpr/cond/branch_0_fun/hgrk,khd->rhgd/dot_general | solution.py:43
  218.5 7.9 %conditional.2 = (f32[1,4,384]{2,1,0:T(4,128)S(1)}, f32[1,4,384]{2,1,0:T(4,128)S(1)}, f32[384,1,4,128]{0,3,2,1:T(8,128)S(1)}) conditional(s32[]{:T(128)} %convert_element_type.58, (s32[1,1536]{1,0:T(1,128)S(1)}, s32[384]{0:T(512)S(1)}, bf16[8,1536,1,128]{3,1,2,0:T(8,128)(2,1)}, s32[]{:T(128)}, bf16[384,1,4,128]{3,0,2,1:T(8,128)(2,1)S(1)}, ...), branch_computations={%region_3.5_spmd, %region_6.6_spmd} | conditional | flops 1227821568 | bytes 33530396 | solution.py:89
  219.0 2.5 fusion
  223.2 3.2 %fusion.12 = f32[384,1,4,128]{0,3,2,1:T(8,128)S(1)} fusion(f32[1536,384,4]{1,0,2:T(8,128)S(1)} %get-tuple-element.191, f32[4,384]{1,0:T(4,128)S(1)} %bitcast.84, pred[384,1536]{0,1:T(8,128)(4,1)S(1)} %broadcast_compare_fusion, f32[384,1,4,128]{0,3,2,1:T(8,128)S(1)} %get-tuple-element.124, bf16[8,1536,1,128]{1,3,2,0:T(8,128)(2,1)} %get-tuple-element.125, ...), kind=kOutput, calls=%fused_computation.12 | convolution fusion | flops 611450880 | bytes 12005888 | tf_op jit(solution)/shard_map/while/body/eval_jaxpr/cond/branch_0_fun/hgrk,khd->rhgd/dot_general | solution.py:43
  228.3 7.9 %conditional.2 = (f32[1,4,384]{2,1,0:T(4,128)S(1)}, f32[1,4,384]{2,1,0:T(4,128)S(1)}, f32[384,1,4,128]{0,3,2,1:T(8,128)S(1)}) conditional(s32[]{:T(128)} %convert_element_type.58, (s32[1,1536]{1,0:T(1,128)S(1)}, s32[384]{0:T(512)S(1)}, bf16[8,1536,1,128]{3,1,2,0:T(8,128)(2,1)}, s32[]{:T(128)}, bf16[384,1,4,128]{3,0,2,1:T(8,128)(2,1)S(1)}, ...), branch_computations={%region_3.5_spmd, %region_6.6_spmd} | conditional | flops 1227821568 | bytes 33530396 | solution.py:89
  233.0 3.2 %fusion.12 = f32[384,1,4,128]{0,3,2,1:T(8,128)S(1)} fusion(f32[1536,384,4]{1,0,2:T(8,128)S(1)} %get-tuple-element.191, f32[4,384]{1,0:T(4,128)S(1)} %bitcast.84, pred[384,1536]{0,1:T(8,128)(4,1)S(1)} %broadcast_compare_fusion, f32[384,1,4,128]{0,3,2,1:T(8,128)S(1)} %get-tuple-element.124, bf16[8,1536,1,128]{1,3,2,0:T(8,128)(2,1)} %get-tuple-element.125, ...), kind=kOutput, calls=%fused_computation.12 | convolution fusion | flops 611450880 | bytes 12005888 | tf_op jit(solution)/shard_map/while/body/eval_jaxpr/cond/branch_0_fun/hgrk,khd->rhgd/dot_general | solution.py:43
  238.2 7.9 %conditional.2 = (f32[1,4,384]{2,1,0:T(4,128)S(1)}, f32[1,4,384]{2,1,0:T(4,128)S(1)}, f32[384,1,4,128]{0,3,2,1:T(8,128)S(1)}) conditional(s32[]{:T(128)} %convert_element_type.58, (s32[1,1536]{1,0:T(1,128)S(1)}, s32[384]{0:T(512)S(1)}, bf16[8,1536,1,128]{3,1,2,0:T(8,128)(2,1)}, s32[]{:T(128)}, bf16[384,1,4,128]{3,0,2,1:T(8,128)(2,1)S(1)}, ...), branch_computations={%region_3.5_spmd, %region_6.6_spmd} | conditional | flops 1227821568 | bytes 33530396 | solution.py:89
  242.8 3.2 %fusion.12 = f32[384,1,4,128]{0,3,2,1:T(8,128)S(1)} fusion(f32[1536,384,4]{1,0,2:T(8,128)S(1)} %get-tuple-element.191, f32[4,384]{1,0:T(4,128)S(1)} %bitcast.84, pred[384,1536]{0,1:T(8,128)(4,1)S(1)} %broadcast_compare_fusion, f32[384,1,4,128]{0,3,2,1:T(8,128)S(1)} %get-tuple-element.124, bf16[8,1536,1,128]{1,3,2,0:T(8,128)(2,1)} %get-tuple-element.125, ...), kind=kOutput, calls=%fused_computation.12 | convolution fusion | flops 611450880 | bytes 12005888 | tf_op jit(solution)/shard_map/while/body/eval_jaxpr/cond/branch_0_fun/hgrk,khd->rhgd/dot_general | solution.py:43
  (94 shorter events, 37.7 us)
Async XLA Ops:
  6.5 1.6 copy-start
  6.5 51.5 %copy-start.1 = (bf16[4096,128]{1,0:T(8,128)(2,1)S(1)}, bf16[4096,128]{1,0:T(8,128)(2,1)}, u32[]{:S(2)}) copy-start(bf16[4096,128]{1,0:T(8,128)(2,1)} %param.15) | copy-start | bytes 3145732
  6.5 51.5 %all-gather.9.cloned.1.call-start = ((), (), s32[]{:S(2)}) async-start(), calls=%async_computation.1 | async-start | bytes 3538944 | tf_op jit(solution)/shard_map/all_gather | solution.py:110
  10.7 98.6 %all-gather.11.cloned.1.call-start = ((), (), s32[]{:S(2)}) async-start(), calls=%async_computation.2 | async-start | bytes 3244032 | tf_op jit(solution)/shard_map/all_gather | solution.py:127
  61.6 28.9 %copy-start.2 = (s32[384]{0:T(512)S(1)}, s32[384]{0:T(512)}, u32[]{:S(2)}) copy-start(s32[384]{0:T(512)} %param.11) | copy-start | bytes 4612
  61.6 28.9 %copy-start.3 = (f32[384]{0:T(512)S(1)}, f32[384]{0:T(512)}, u32[]{:S(2)}) copy-start(f32[384]{0:T(512)} %param.12) | copy-start | bytes 4612
  61.6 101.2 %all-gather.7.cloned.1.call-start = ((), (), s32[]{:S(2)}) async-start(), calls=%async_computation | async-start | bytes 3244032 | tf_op jit(solution)/shard_map/all_gather | solution.py:126
Sparse Core Ops, SparseCore 0:
  10.9 47.1 all-gather.8
  61.7 47.5 all-gather.10
  111.8 51.0 all-gather.6
where the time goes:
time: 255 us; the launch traced here: 254 us
  waiting for transfers between devices  106 us (42%)
  matrix products  57.8 us (23%)
  other arithmetic  26.3 us (10%)
  blocking collectives  23.6 us (9%)
  local copies, waits for them, and re-layouts  15.5 us (6%)
  between operations  13.2 us (5%)
  loops' own time  10.8 us (4%)
    all_gather x1, waiting for transfers between devices, body(): lax.all_gather(key_rows, 'ctx', axis=0, tiled=True)  48.9 us
    all_gather x1, waiting for transfers between devices, body(): piece = lax.all_gather(picked, 'tp', axis=1, tiled=True)  47.3 us
    dot_general x8, matrix products, update(): jnp.einsum('hgrk,khd->rhgd', weights.astype(jnp.bfloat16), value_block, p...  25.3 us
    all_gather x1, blocking collectives, body(): lax.all_gather(position, 'ctx', axis=0, tiled=True)  23.6 us
    dot_general x8, matrix products, update(): jnp.einsum('rhgd,khd->hgrk', queries, key_block, preferred_element_type=j...  20.1 us
    reduce_sum x8, other arithmetic, update(): totals = totals * factor + jnp.sum(weights, axis=-1)  13.6 us
    another operation x1, loops' own time, fold_keys(): result, unused = lax.scan(advance, tuple(states), shaped)  10.4 us
    all_gather x1, waiting for transfers between devices, body(): lax.all_gather(value_rows, 'ctx', axis=0, tiled=True)  9.97 us
  transfers between devices with their start and end apart: 3, of which 3 were waited for; matrix products, arithmetic and copies ran while one was open for 7% of the time, Pallas kernels for 0%

commit v1 on v0

--- a/solution.py
+++ b/solution.py
@@ -107,7 +107,9 @@
     position = jnp.where(live, lax.axis_index("ctx") * seq_rows + chosen, pad_mark)
     picked = hidden_states[jnp.minimum(chosen, seq_rows - 1)]
     gated = jnp.where(live, router_gate, 0.0)
-    piece = lax.all_gather(picked, "tp", axis=1, tiled=True)
+    piece = jnp.concatenate(
+        lax.all_to_all(jnp.stack([picked] * lax.axis_size("tp")), "tp", 0, 0), axis=1
+    )
     query_part = jnp.dot(piece, w_query, preferred_element_type=jnp.float32)
     key_part = jnp.dot(piece, w_key, preferred_element_type=jnp.float32)
     value_part = jnp.dot(piece, w_value, preferred_element_type=jnp.float32)

time: 255 us -> 288 us (1.13)
  blocking collectives: 23.6 us -> 105 us
  waiting for transfers between devices: 106 us -> 41.4 us
  local copies, waits for them, and re-layouts: 15.5 us -> 34.7 us
    all_to_all x0 -> x1, blocking collectives: none -> 80.3 us  [body(): lax.all_to_all(jnp.stack([picked] * lax.axis_size('tp')), 'tp', 0, 0)]
    all_gather x1 -> x0, waiting for transfers between devices: 47.3 us -> none  [body(): piece = lax.all_gather(picked, 'tp', axis=1, tiled=True)]
    reshape x1 -> x3, local copies, waits for them, and re-layouts: 1.39 us -> 11.7 us  [body(): jnp.concatenate(lax.all_to_all(jnp.stack([picked] * lax.axis_size('tp')),...]
    all_gather x1, waiting for transfers between devices: 9.97 us -> 0.02 us  [body(): lax.all_gather(value_rows, 'ctx', axis=0, tiled=True)]
    all_gather x1, waiting for transfers between devices: 48.9 us -> 41.3 us  [body(): lax.all_gather(key_rows, 'ctx', axis=0, tiled=True)]
    dot_general x0 -> x1, local copies, waits for them, and re-layouts: none -> 6.45 us  [body(): query_part = jnp.dot(piece, w_query, preferred_element_type=jnp.float32)]
    unnamed x9 -> x15, local copies, waits for them, and re-layouts: 0.77 us -> 3.73 us
    while x2 -> x3, local copies, waits for them, and re-layouts: 9.28 us -> 9.52 us  [fold_keys(): result, unused = lax.scan(advance, tuple(states), shaped)]
  transfers between devices with their start and end apart: 3 -> 2, of which waited for: 3 -> 1; matrix products, arithmetic and copies ran while one was open for 7% -> 12% of each run, Pallas kernels for 0% -> 0%
where the time goes in v1:
time: 288 us; the launch traced here: 287 us
  blocking collectives  105 us (36%)
  matrix products  55.3 us (19%)
  waiting for transfers between devices  41.4 us (14%)
  local copies, waits for them, and re-layouts  34.7 us (12%)
  other arithmetic  25.7 us (9%)
  between operations  13.6 us (5%)
  loops' own time  10.9 us (4%)
    all_to_all x1, blocking collectives, body(): lax.all_to_all(jnp.stack([picked] * lax.axis_size('tp')), 'tp', 0, 0)  80.3 us
    all_gather x1, waiting for transfers between devices, body(): lax.all_gather(key_rows, 'ctx', axis=0, tiled=True)  41.3 us
    dot_general x8, matrix products, update(): jnp.einsum('hgrk,khd->rhgd', weights.astype(jnp.bfloat16), value_block, p...  25.2 us
    all_gather x1, blocking collectives, body(): lax.all_gather(position, 'ctx', axis=0, tiled=True)  24.8 us
    dot_general x8, matrix products, update(): jnp.einsum('rhgd,khd->hgrk', queries, key_block, preferred_element_type=j...  20.1 us
    reduce_sum x8, other arithmetic, update(): totals = totals * factor + jnp.sum(weights, axis=-1)  13.6 us
    reshape x3, local copies, waits for them, and re-layouts, body(): jnp.concatenate(lax.all_to_all(jnp.stack([picked] * lax.axis_size('tp')),...  11.7 us
    another operation x1, loops' own time, fold_keys(): result, unused = lax.scan(advance, tuple(states), shaped)  10.5 us
  transfers between devices with their start and end apart: 2, of which 1 were waited for; matrix products, arithmetic and copies ran while one was open for 12% of the time, Pallas kernels for 0%

profile of v1, /device:TPU:23, one launch (start us, length us, event | category | flops | bytes accessed | tf_op | source)
XLA Modules:
  0.0 286.8 jit_solution(10068599358649758571)
XLA Ops:
  10.5 80.3 %all_to_all.5 = bf16[8,384,512]{2,1,0:T(8,128)(2,1)S(1)} all-to-all(bf16[8,384,512]{2,1,0:T(8,128)(2,1)S(1)} %stack.2), channel_id=1, replica_groups=mesh['ctx'=32,'tp'=8] {'tp'}, dimensions={0} | all-to-all | bytes 6291456 | tf_op jit(solution)/shard_map/all_to_all | solution.py:111
  95.9 2.9 %convolution_bitcast_fusion = f32[384,1,128]{0,2,1:T(8,128)S(1)} fusion(bf16[384,4096]{1,0:T(8,128)(2,1)} %bitcast.89, bf16[4096,128]{1,0:T(8,128)(2,1)S(1)} %copy-done.4), kind=kOutput, calls=%fused_computation.28 | convolution fusion | flops 402653184 | bytes 4390912 | tf_op jit(solution)/shard_map/dot_general | solution.py:114
  99.9 6.4 %copy.22 = bf16[512,4096]{1,0:T(8,128)(2,1)} copy(bf16[512,4096]{0,1:T(8,128)(2,1)} %bitcast.91) | data formatting | bytes 8388608 | tf_op jit(solution)/shard_map/dot_general | solution.py:113
  106.4 24.8 %all-gather.1 = s32[32,1,384]{2,1,0:T(1,128)S(1)} all-gather(s32[1,1,384]{2,1,0:T(1,128)S(1)} %reshape.294), channel_id=1, replica_groups=mesh['ctx'=32,'tp'=8] {'ctx'}, dimensions={0}, use_global_device_ids=true | all-gather | bytes 50688 | tf_op jit(solution)/shard_map/all_gather | solution.py:130
  132.4 5.4 %copy.14 = bf16[384,8,512]{2,1,0:T(8,128)(2,1)} copy(bf16[384,8,512]{2,0,1:T(8,128)(2,1)} %bitcast.87) | data formatting | bytes 6291456 | tf_op jit(solution)/shard_map/reshape | solution.py:110
  137.8 5.9 %reshape.299 = bf16[384,4096,1]{1,0,2:T(8,128)(2,1)} reshape(bf16[384,8,512]{2,1,0:T(8,128)(2,1)} %copy.14) | data formatting | bytes 6291456 | tf_op jit(solution)/shard_map/reshape | solution.py:110
  143.7 5.5 %fusion.38 = f32[384,4,128]{0,2,1:T(8,128)S(1)} fusion(bf16[384,4096,1]{1,0,2:T(8,128)(2,1)} %reshape.299, bf16[4,128,4096]{2,1,0:T(8,128)(2,1)} %bitcast.92), kind=kOutput, calls=%fused_computation.60 | convolution fusion | flops 1610612736 | bytes 8126464 | tf_op jit(solution)/shard_map/dot_general | solution.py:113
  149.6 4.7 %copy.18 = bf16[8,1536,1,128]{1,3,2,0:T(8,128)(2,1)} copy(bf16[8,1536,1,128]{3,1,0,2:T(8,128)(2,1)} %bitcast.93) | data formatting | bytes 6291456 | tf_op jit(solution)/shard_map/while | solution.py:92
  154.3 41.3 %all-gather.5.cloned.1.call-done = bf16[12288,1,128]{0,2,1:T(8,128)(2,1)} async-done(((bf16[384,1,128]{0,2,1:T(8,128)(2,1)}), bf16[12288,1,128]{0,2,1:T(8,128)(2,1)}) %all-gather.5.cloned.1.call-update) | async-done | bytes 3145744 | tf_op jit(solution)/shard_map/all_gather | solution.py:128
  195.6 4.6 %copy.21 = bf16[12288,1,128]{2,0,1:T(8,128)(2,1)} copy(bf16[12288,1,128]{0,2,1:T(8,128)(2,1)} %all-gather.5.cloned.1.call-done) | data formatting | bytes 6291456 | tf_op jit(solution)/shard_map/while | solution.py:92
  200.3 78.6 %while.14 = (s32[]{:T(128)}, f32[1,4,384]{2,1,0:T(4,128)S(1)}, f32[1,4,384]{2,1,0:T(4,128)S(1)}, f32[384,1,4,128]{0,3,2,1:T(8,128)S(1)}, s32[8,1536]{1,0:T(8,128...) while((s32[]{:T(128)}, f32[1,4,384]{2,1,0:T(4,128)S(1)}, ...), condition=%wide.region_7.8_spmd, body=%wide.region_1.7_spmd.sunk | while | flops 1227823104 | bytes 33555200 | solution.py:92
  202.3 7.9 %conditional.2 = (f32[1,4,384]{2,1,0:T(4,128)S(1)}, f32[1,4,384]{2,1,0:T(4,128)S(1)}, f32[384,1,4,128]{0,3,2,1:T(8,128)S(1)}) conditional(s32[]{:T(128)} %convert_element_type.58, (s32[1,1536]{1,0:T(1,128)S(1)}, s32[384]{0:T(512)S(1)}, bf16[8,1536,1,128]{3,1,2,0:T(8,128)(2,1)}, s32[]{:T(128)}, bf16[384,1,4,128]{3,0,2,1:T(8,128)(2,1)S(1)}, ...), branch_computations={%region_3.5_spmd, %region_6.6_spmd} | conditional | flops 1227821568 | bytes 33530396 | solution.py:89
  202.7 2.5 fusion
  206.9 3.2 %fusion.12 = f32[384,1,4,128]{0,3,2,1:T(8,128)S(1)} fusion(f32[1536,384,4]{1,0,2:T(8,128)S(1)} %get-tuple-element.191, f32[4,384]{1,0:T(4,128)S(1)} %bitcast.95, pred[384,1536]{0,1:T(8,128)(4,1)S(1)} %broadcast_compare_fusion, f32[384,1,4,128]{0,3,2,1:T(8,128)S(1)} %get-tuple-element.124, bf16[8,1536,1,128]{1,3,2,0:T(8,128)(2,1)} %get-tuple-element.125, ...), kind=kOutput, calls=%fused_computation.12 | convolution fusion | flops 611450880 | bytes 12005888 | tf_op jit(solution)/shard_map/while/body/eval_jaxpr/cond/branch_0_fun/hgrk,khd->rhgd/dot_general | solution.py:43
  212.1 7.9 %conditional.2 = (f32[1,4,384]{2,1,0:T(4,128)S(1)}, f32[1,4,384]{2,1,0:T(4,128)S(1)}, f32[384,1,4,128]{0,3,2,1:T(8,128)S(1)}) conditional(s32[]{:T(128)} %convert_element_type.58, (s32[1,1536]{1,0:T(1,128)S(1)}, s32[384]{0:T(512)S(1)}, bf16[8,1536,1,128]{3,1,2,0:T(8,128)(2,1)}, s32[]{:T(128)}, bf16[384,1,4,128]{3,0,2,1:T(8,128)(2,1)S(1)}, ...), branch_computations={%region_3.5_spmd, %region_6.6_spmd} | conditional | flops 1227821568 | bytes 33530396 | solution.py:89
  212.5 2.5 fusion
  216.8 3.2 %fusion.12 = f32[384,1,4,128]{0,3,2,1:T(8,128)S(1)} fusion(f32[1536,384,4]{1,0,2:T(8,128)S(1)} %get-tuple-element.191, f32[4,384]{1,0:T(4,128)S(1)} %bitcast.95, pred[384,1536]{0,1:T(8,128)(4,1)S(1)} %broadcast_compare_fusion, f32[384,1,4,128]{0,3,2,1:T(8,128)S(1)} %get-tuple-element.124, bf16[8,1536,1,128]{1,3,2,0:T(8,128)(2,1)} %get-tuple-element.125, ...), kind=kOutput, calls=%fused_computation.12 | convolution fusion | flops 611450880 | bytes 12005888 | tf_op jit(solution)/shard_map/while/body/eval_jaxpr/cond/branch_0_fun/hgrk,khd->rhgd/dot_general | solution.py:43
  221.9 7.9 %conditional.2 = (f32[1,4,384]{2,1,0:T(4,128)S(1)}, f32[1,4,384]{2,1,0:T(4,128)S(1)}, f32[384,1,4,128]{0,3,2,1:T(8,128)S(1)}) conditional(s32[]{:T(128)} %convert_element_type.58, (s32[1,1536]{1,0:T(1,128)S(1)}, s32[384]{0:T(512)S(1)}, bf16[8,1536,1,128]{3,1,2,0:T(8,128)(2,1)}, s32[]{:T(128)}, bf16[384,1,4,128]{3,0,2,1:T(8,128)(2,1)S(1)}, ...), branch_computations={%region_3.5_spmd, %region_6.6_spmd} | conditional | flops 1227821568 | bytes 33530396 | solution.py:89
  226.6 3.2 %fusion.12 = f32[384,1,4,128]{0,3,2,1:T(8,128)S(1)} fusion(f32[1536,384,4]{1,0,2:T(8,128)S(1)} %get-tuple-element.191, f32[4,384]{1,0:T(4,128)S(1)} %bitcast.95, pred[384,1536]{0,1:T(8,128)(4,1)S(1)} %broadcast_compare_fusion, f32[384,1,4,128]{0,3,2,1:T(8,128)S(1)} %get-tuple-element.124, bf16[8,1536,1,128]{1,3,2,0:T(8,128)(2,1)} %get-tuple-element.125, ...), kind=kOutput, calls=%fused_computation.12 | convolution fusion | flops 611450880 | bytes 12005888 | tf_op jit(solution)/shard_map/while/body/eval_jaxpr/cond/branch_0_fun/hgrk,khd->rhgd/dot_general | solution.py:43
  231.7 7.9 %conditional.2 = (f32[1,4,384]{2,1,0:T(4,128)S(1)}, f32[1,4,384]{2,1,0:T(4,128)S(1)}, f32[384,1,4,128]{0,3,2,1:T(8,128)S(1)}) conditional(s32[]{:T(128)} %convert_element_type.58, (s32[1,1536]{1,0:T(1,128)S(1)}, s32[384]{0:T(512)S(1)}, bf16[8,1536,1,128]{3,1,2,0:T(8,128)(2,1)}, s32[]{:T(128)}, bf16[384,1,4,128]{3,0,2,1:T(8,128)(2,1)S(1)}, ...), branch_computations={%region_3.5_spmd, %region_6.6_spmd} | conditional | flops 1227821568 | bytes 33530396 | solution.py:89
  232.2 2.5 fusion
  236.4 3.2 %fusion.12 = f32[384,1,4,128]{0,3,2,1:T(8,128)S(1)} fusion(f32[1536,384,4]{1,0,2:T(8,128)S(1)} %get-tuple-element.191, f32[4,384]{1,0:T(4,128)S(1)} %bitcast.95, pred[384,1536]{0,1:T(8,128)(4,1)S(1)} %broadcast_compare_fusion, f32[384,1,4,128]{0,3,2,1:T(8,128)S(1)} %get-tuple-element.124, bf16[8,1536,1,128]{1,3,2,0:T(8,128)(2,1)} %get-tuple-element.125, ...), kind=kOutput, calls=%fused_computation.12 | convolution fusion | flops 611450880 | bytes 12005888 | tf_op jit(solution)/shard_map/while/body/eval_jaxpr/cond/branch_0_fun/hgrk,khd->rhgd/dot_general | solution.py:43
  241.5 7.9 %conditional.2 = (f32[1,4,384]{2,1,0:T(4,128)S(1)}, f32[1,4,384]{2,1,0:T(4,128)S(1)}, f32[384,1,4,128]{0,3,2,1:T(8,128)S(1)}) conditional(s32[]{:T(128)} %convert_element_type.58, (s32[1,1536]{1,0:T(1,128)S(1)}, s32[384]{0:T(512)S(1)}, bf16[8,1536,1,128]{3,1,2,0:T(8,128)(2,1)}, s32[]{:T(128)}, bf16[384,1,4,128]{3,0,2,1:T(8,128)(2,1)S(1)}, ...), branch_computations={%region_3.5_spmd, %region_6.6_spmd} | conditional | flops 1227821568 | bytes 33530396 | solution.py:89
  246.2 3.2 %fusion.12 = f32[384,1,4,128]{0,3,2,1:T(8,128)S(1)} fusion(f32[1536,384,4]{1,0,2:T(8,128)S(1)} %get-tuple-element.191, f32[4,384]{1,0:T(4,128)S(1)} %bitcast.95, pred[384,1536]{0,1:T(8,128)(4,1)S(1)} %broadcast_compare_fusion, f32[384,1,4,128]{0,3,2,1:T(8,128)S(1)} %get-tuple-element.124, bf16[8,1536,1,128]{1,3,2,0:T(8,128)(2,1)} %get-tuple-element.125, ...), kind=kOutput, calls=%fused_computation.12 | convolution fusion | flops 611450880 | bytes 12005888 | tf_op jit(solution)/shard_map/while/body/eval_jaxpr/cond/branch_0_fun/hgrk,khd->rhgd/dot_general | solution.py:43
  251.4 7.9 %conditional.2 = (f32[1,4,384]{2,1,0:T(4,128)S(1)}, f32[1,4,384]{2,1,0:T(4,128)S(1)}, f32[384,1,4,128]{0,3,2,1:T(8,128)S(1)}) conditional(s32[]{:T(128)} %convert_element_type.58, (s32[1,1536]{1,0:T(1,128)S(1)}, s32[384]{0:T(512)S(1)}, bf16[8,1536,1,128]{3,1,2,0:T(8,128)(2,1)}, s32[]{:T(128)}, bf16[384,1,4,128]{3,0,2,1:T(8,128)(2,1)S(1)}, ...), branch_computations={%region_3.5_spmd, %region_6.6_spmd} | conditional | flops 1227821568 | bytes 33530396 | solution.py:89
  251.8 2.5 fusion
  256.0 3.2 %fusion.12 = f32[384,1,4,128]{0,3,2,1:T(8,128)S(1)} fusion(f32[1536,384,4]{1,0,2:T(8,128)S(1)} %get-tuple-element.191, f32[4,384]{1,0:T(4,128)S(1)} %bitcast.95, pred[384,1536]{0,1:T(8,128)(4,1)S(1)} %broadcast_compare_fusion, f32[384,1,4,128]{0,3,2,1:T(8,128)S(1)} %get-tuple-element.124, bf16[8,1536,1,128]{1,3,2,0:T(8,128)(2,1)} %get-tuple-element.125, ...), kind=kOutput, calls=%fused_computation.12 | convolution fusion | flops 611450880 | bytes 12005888 | tf_op jit(solution)/shard_map/while/body/eval_jaxpr/cond/branch_0_fun/hgrk,khd->rhgd/dot_general | solution.py:43
  261.2 7.9 %conditional.2 = (f32[1,4,384]{2,1,0:T(4,128)S(1)}, f32[1,4,384]{2,1,0:T(4,128)S(1)}, f32[384,1,4,128]{0,3,2,1:T(8,128)S(1)}) conditional(s32[]{:T(128)} %convert_element_type.58, (s32[1,1536]{1,0:T(1,128)S(1)}, s32[384]{0:T(512)S(1)}, bf16[8,1536,1,128]{3,1,2,0:T(8,128)(2,1)}, s32[]{:T(128)}, bf16[384,1,4,128]{3,0,2,1:T(8,128)(2,1)S(1)}, ...), branch_computations={%region_3.5_spmd, %region_6.6_spmd} | conditional | flops 1227821568 | bytes 33530396 | solution.py:89
  265.9 3.2 %fusion.12 = f32[384,1,4,128]{0,3,2,1:T(8,128)S(1)} fusion(f32[1536,384,4]{1,0,2:T(8,128)S(1)} %get-tuple-element.191, f32[4,384]{1,0:T(4,128)S(1)} %bitcast.95, pred[384,1536]{0,1:T(8,128)(4,1)S(1)} %broadcast_compare_fusion, f32[384,1,4,128]{0,3,2,1:T(8,128)S(1)} %get-tuple-element.124, bf16[8,1536,1,128]{1,3,2,0:T(8,128)(2,1)} %get-tuple-element.125, ...), kind=kOutput, calls=%fused_computation.12 | convolution fusion | flops 611450880 | bytes 12005888 | tf_op jit(solution)/shard_map/while/body/eval_jaxpr/cond/branch_0_fun/hgrk,khd->rhgd/dot_general | solution.py:43
  271.0 7.9 %conditional.2 = (f32[1,4,384]{2,1,0:T(4,128)S(1)}, f32[1,4,384]{2,1,0:T(4,128)S(1)}, f32[384,1,4,128]{0,3,2,1:T(8,128)S(1)}) conditional(s32[]{:T(128)} %convert_element_type.58, (s32[1,1536]{1,0:T(1,128)S(1)}, s32[384]{0:T(512)S(1)}, bf16[8,1536,1,128]{3,1,2,0:T(8,128)(2,1)}, s32[]{:T(128)}, bf16[384,1,4,128]{3,0,2,1:T(8,128)(2,1)S(1)}, ...), branch_computations={%region_3.5_spmd, %region_6.6_spmd} | conditional | flops 1227821568 | bytes 33530396 | solution.py:89
  271.4 2.5 fusion
  275.7 3.2 %fusion.12 = f32[384,1,4,128]{0,3,2,1:T(8,128)S(1)} fusion(f32[1536,384,4]{1,0,2:T(8,128)S(1)} %get-tuple-element.191, f32[4,384]{1,0:T(4,128)S(1)} %bitcast.95, pred[384,1536]{0,1:T(8,128)(4,1)S(1)} %broadcast_compare_fusion, f32[384,1,4,128]{0,3,2,1:T(8,128)S(1)} %get-tuple-element.124, bf16[8,1536,1,128]{1,3,2,0:T(8,128)(2,1)} %get-tuple-element.125, ...), kind=kOutput, calls=%fused_computation.12 | convolution fusion | flops 611450880 | bytes 12005888 | tf_op jit(solution)/shard_map/while/body/eval_jaxpr/cond/branch_0_fun/hgrk,khd->rhgd/dot_general | solution.py:43
  (102 shorter events, 42.7 us)
Async XLA Ops:
  6.5 1.6 copy-start
  6.5 143.1 %all-gather.7.cloned.1.call-start = ((), (), s32[]{:S(2)}) async-start(), calls=%async_computation.2 | async-start | bytes 3244032 | tf_op jit(solution)/shard_map/all_gather | solution.py:129
  90.8 1.7 copy-start.1
  90.8 3.4 %copy-start.3 = (bf16[4096,128]{1,0:T(8,128)(2,1)S(1)}, bf16[4096,128]{1,0:T(8,128)(2,1)}, u32[]{:S(2)}) copy-start(bf16[4096,128]{1,0:T(8,128)(2,1)} %param.15) | copy-start | bytes 3145732
  92.5 1.6 copy-start.2
  92.5 3.4 %copy-start.4 = (bf16[4096,128]{1,0:T(8,128)(2,1)S(1)}, bf16[4096,128]{1,0:T(8,128)(2,1)}, u32[]{:S(2)}) copy-start(bf16[4096,128]{1,0:T(8,128)(2,1)} %param.14) | copy-start | bytes 3145732
  95.8 99.8 %all-gather.5.cloned.1.call-start = ((), (), s32[]{:S(2)}) async-start(), calls=%async_computation.1 | async-start | bytes 3244032 | tf_op jit(solution)/shard_map/all_gather | solution.py:128
  99.9 32.1 %copy-start.5 = (s32[384]{0:T(512)S(1)}, s32[384]{0:T(512)}, u32[]{:S(2)}) copy-start(s32[384]{0:T(512)} %param.11) | copy-start | bytes 4612
  99.9 32.1 %copy-start.6 = (f32[384]{0:T(512)S(1)}, f32[384]{0:T(512)}, u32[]{:S(2)}) copy-start(f32[384]{0:T(512)} %param.12) | copy-start | bytes 4612
Sparse Core Ops, SparseCore 0:
  95.9 46.1 all-gather.6
  144.5 51.0 all-gather.4
